TPU v7x, 32 devices: a whole 2x2x4 slice. The times are simulated.
32 devices in a mesh: row: 4 (over y, core), col: 8 (over z, x).
Axes of the slice: x: 2, y: 2, z: 4, core: 2. Of those that a mesh axis runs over, the one named last changes fastest.
Arguments:
- bands: float32 [2, 12, 32, 1024], P(None, None, 'row', 'col'), may hold values from -500 to 500
- directions: float32 [2, 12, 32, 1024], P(None, None, 'row', 'col'), may hold values from -500 to 500
- materials: int32 [32, 1024], P('row', 'col'), may hold values from 0 to 7
- permittivity: float32 [8], replicated, may hold values from 1 to 12
- wavevector: int32 [2], replicated, may hold values from 0 to 15
Outputs:
- basis: float32 [2, 36, 32, 1024], P(None, None, 'row', 'col')
- reduced: float32 [2, 36, 36], replicated
All inputs are finite; a program needn't handle non-finite values.
Results may differ from a plain program's by a relative error of at most 0.00018.
Values sent between devices are 32-bit elements; how exact they have to be, the bound alone decides.
No kernel may reach another device: no remote copies, remote signals or barrier semaphores. Data moves between devices by JAX's collectives and lax.ppermute only.
A program may use at most 64 MiB of HBM per device.

v0:
```python
import math
import jax
import jax.numpy as jnp
from jax import lax
from jax.sharding import PartitionSpec as P

KDEN = 16
NS_STEPS = 5


def with_halo(cells, sides, width):
    for axis, dim in sides:
        count = lax.axis_size(axis)
        head = lax.slice_in_dim(cells, 0, width, axis=dim)
        tail = lax.slice_in_dim(cells, cells.shape[dim] - width, cells.shape[dim], axis=dim)
        cells = jnp.concatenate(
            [
                lax.ppermute(tail, axis, [(i, (i + 1) % count) for i in range(count)]),
                cells,
                lax.ppermute(head, axis, [((i + 1) % count, i) for i in range(count)]),
            ],
            axis=dim,
        )
    return cells


def rotate(values, phase_angle):
    cosine = jnp.cos(phase_angle)
    sine_part = jnp.sin(phase_angle)
    return jnp.stack(
        [values[0] * cosine - values[1] * sine_part, values[0] * sine_part + values[1] * cosine]
    )


def bloch_rims(padded, edges, rim_layers):
    low_row, high_row, low_col, high_col = edges
    padded = padded.at[:, :, :rim_layers].set(rotate(padded[:, :, :rim_layers], low_row))
    padded = padded.at[:, :, -rim_layers:].set(rotate(padded[:, :, -rim_layers:], high_row))
    padded = padded.at[:, :, :, :rim_layers].set(rotate(padded[:, :, :, :rim_layers], low_col))
    padded = padded.at[:, :, :, -rim_layers:].set(rotate(padded[:, :, :, -rim_layers:], high_col))
    return padded


def stencil(padded, stiff_pad):
    centre = stiff_pad[1:-1, 1:-1]
    upward = 0.5 * (centre + stiff_pad[:-2, 1:-1])
    downward = 0.5 * (centre + stiff_pad[2:, 1:-1])
    leftward = 0.5 * (centre + stiff_pad[1:-1, :-2])
    rightward = 0.5 * (centre + stiff_pad[1:-1, 2:])
    diagonal = upward + downward + leftward + rightward
    inner_cells = padded[:, :, 1:-1, 1:-1]
    neighbours = (
        upward * padded[:, :, :-2, 1:-1]
        + downward * padded[:, :, 2:, 1:-1]
        + leftward * padded[:, :, 1:-1, :-2]
        + rightward * padded[:, :, 1:-1, 2:]
    )
    return (diagonal * inner_cells - neighbours, diagonal)


def complex_gram(first_block, second_block):
    highest = lax.Precision.HIGHEST
    first_flat = first_block.reshape(first_block.shape[0], first_block.shape[1], -1)
    second_flat = second_block.reshape(second_block.shape[0], second_block.shape[1], -1)
    real_part = jnp.einsum("pjc,pkc->jk", first_flat, second_flat, precision=highest)
    imag_part = jnp.einsum(
        "jc,kc->jk", first_flat[0], second_flat[1], precision=highest
    ) - jnp.einsum("jc,kc->jk", first_flat[1], second_flat[0], precision=highest)
    return (real_part, imag_part)


def inverse_root(gram_real, gram_imag):
    highest = lax.Precision.HIGHEST
    order_size = gram_real.shape[0]
    upper_half = jnp.concatenate([gram_real, -gram_imag], axis=1)
    lower_half = jnp.concatenate([gram_imag, gram_real], axis=1)
    embedded = jnp.concatenate([upper_half, lower_half], axis=0)
    magnitude = jnp.sqrt(jnp.sum(embedded * embedded))
    identity = jnp.eye(2 * order_size, dtype=embedded.dtype)

    def newton(turn_index, carried):
        current, inverse = carried
        factor = 1.5 * identity - 0.5 * jnp.dot(inverse, current, precision=highest)
        return (
            jnp.dot(current, factor, precision=highest),
            jnp.dot(factor, inverse, precision=highest),
        )

    current, inverse = lax.fori_loop(0, NS_STEPS, newton, (embedded / magnitude, identity))
    root_full = inverse / jnp.sqrt(magnitude)
    return (root_full[:order_size, :order_size], root_full[order_size:, :order_size])


def reduce_matrix(root_real, root_imag, ham_real, ham_imag):
    highest = lax.Precision.HIGHEST
    prod_real = jnp.dot(ham_real, root_real, precision=highest) - jnp.dot(
        ham_imag, root_imag, precision=highest
    )
    prod_imag = jnp.dot(ham_real, root_imag, precision=highest) + jnp.dot(
        ham_imag, root_real, precision=highest
    )
    red_real = jnp.dot(root_real.T, prod_real, precision=highest) + jnp.dot(
        root_imag.T, prod_imag, precision=highest
    )
    red_imag = jnp.dot(root_real.T, prod_imag, precision=highest) - jnp.dot(
        root_imag.T, prod_real, precision=highest
    )
    return jnp.stack([red_real, red_imag])


def rotate_basis(raw_basis, root_real, root_imag, scale_factor):
    highest = lax.Precision.HIGHEST
    basis_real = jnp.einsum("jrc,jk->krc", raw_basis[0], root_real, precision=highest) - jnp.einsum(
        "jrc,jk->krc", raw_basis[1], root_imag, precision=highest
    )
    basis_imag = jnp.einsum("jrc,jk->krc", raw_basis[0], root_imag, precision=highest) + jnp.einsum(
        "jrc,jk->krc", raw_basis[1], root_real, precision=highest
    )
    return scale_factor * jnp.stack([basis_real, basis_imag])


def project_mixing(mixing, matrix):
    highest = lax.Precision.HIGHEST
    return jnp.dot(mixing.T, jnp.dot(matrix, mixing, precision=highest), precision=highest)


def body(bands, directions, materials, permittivity, wavevector):
    band_count = bands.shape[1]
    height = bands.shape[2]
    breadth = bands.shape[3]
    levels = jnp.arange(permittivity.shape[0], dtype=jnp.int32)
    stiffness = jnp.sum(
        jnp.where(
            materials[None] == levels[:, None, None], (1.0 / permittivity)[:, None, None], 0.0
        ),
        axis=0,
    )
    angle_row = 2.0 * math.pi * wavevector[0].astype(jnp.float32) / KDEN
    angle_col = 2.0 * math.pi * wavevector[1].astype(jnp.float32) / KDEN
    row_index = lax.axis_index("row")
    col_index = lax.axis_index("col")
    edges = (
        jnp.where(row_index == 0, -angle_row, 0.0),
        jnp.where(row_index == lax.axis_size("row") - 1, angle_row, 0.0),
        jnp.where(col_index == 0, -angle_col, 0.0),
        jnp.where(col_index == lax.axis_size("col") - 1, angle_col, 0.0),
    )
    packed = jnp.concatenate(
        [bands.reshape(2 * band_count, height, breadth), stiffness[None]], axis=0
    )
    padded = with_halo(packed, (("row", 1), ("col", 2)), 1)
    stiff_cycle = padded[-1]
    band_pad = bloch_rims(padded[:-1].reshape(2, band_count, height + 2, breadth + 2), edges, 1)
    applied_cycle, diagonal_cycle = stencil(band_pad, stiff_cycle)
    scaled_cycle = jnp.concatenate([applied_cycle / diagonal_cycle, bands / diagonal_cycle], axis=1)
    stacked = jnp.concatenate([scaled_cycle, directions], axis=1)
    columns_now = stacked.shape[1]
    field_pad = with_halo(
        stacked.reshape(2 * columns_now, height, breadth), (("row", 1), ("col", 2)), 1
    )
    field_pad = bloch_rims(field_pad.reshape(2, columns_now, height + 2, breadth + 2), edges, 1)
    extra_applied = stencil(field_pad, stiff_cycle)[0]
    scaled_image = scaled_cycle[:, :band_count]
    scaled_bands = scaled_cycle[:, band_count:]
    extra = jnp.concatenate([scaled_image, scaled_bands, directions], axis=1)
    extended = jnp.concatenate([bands, extra], axis=1)
    extended_applied = jnp.concatenate([applied_cycle, extra_applied], axis=1)
    local_gram = complex_gram(extended, extended)
    local_ham = complex_gram(extended, extended_applied)
    gram_whole, gram_imag_whole, ham_whole, ham_imag_whole = lax.psum(
        (local_gram[0], local_gram[1], local_ham[0], local_ham[1]), ("row", "col")
    )
    quotient = jnp.diagonal(ham_whole)[:band_count] / jnp.diagonal(gram_whole)[:band_count]
    identity = jnp.eye(band_count, dtype=jnp.float32)
    zeros_block = jnp.zeros((band_count, band_count), jnp.float32)
    mixing = jnp.concatenate(
        [
            jnp.concatenate([identity, zeros_block, zeros_block], axis=1),
            jnp.concatenate([zeros_block, identity, zeros_block], axis=1),
            jnp.concatenate([zeros_block, -jnp.diag(quotient), zeros_block], axis=1),
            jnp.concatenate([zeros_block, zeros_block, identity], axis=1),
        ],
        axis=0,
    )
    gram_real = project_mixing(mixing, gram_whole)
    gram_imag = project_mixing(mixing, gram_imag_whole)
    ham_real = project_mixing(mixing, ham_whole)
    ham_imag = project_mixing(mixing, ham_imag_whole)
    precond = scaled_image - quotient[None, :, None, None] * scaled_bands
    raw_basis = jnp.concatenate([bands, precond, directions], axis=1)
    root_real, root_imag = inverse_root(gram_real, gram_imag)
    scale_factor = math.sqrt(height * breadth * lax.axis_size("row") * lax.axis_size("col"))
    basis = rotate_basis(raw_basis, root_real, root_imag, scale_factor)
    reduced = reduce_matrix(root_real, root_imag, ham_real, ham_imag)
    return (basis, reduced)


def solution(mesh):
    placed = (P(None, None, "row", "col"), P(None, None, "row", "col"), P("row", "col"), P(), P())
    return jax.shard_map(
        body,
        mesh=mesh,
        in_specs=placed,
        out_specs=(P(None, None, "row", "col"), P()),
        check_vma=False,
    )
```

profile of v0, /device:TPU:0, one launch (start us, length us, event | category | flops | bytes accessed | tf_op | source)
XLA Modules:
  0.0 113.8 jit_solution(13991296870753142769)
XLA Ops:
  0.6 1.0 copy.206
  1.6 0.7 broadcast_divide_fusion.4
  2.3 0.8 select_reduce_fusion
  3.1 0.5 collective-permute-start
  3.6 2.0 %collective-permute-start.1 = (f32[25,1,128]{2,0,1:T(8,128)S(1)}, f32[25,1,128]{2,0,1:T(8,128)S(1)}, u32[]{:S(2)}, u32[]{:S(2)}) collective-permute-start(f32[25,1,128]{2,0,1:T(8,128)S(1)} %get-tuple-element.209), channel_id=1, source_target_pairs={{8,0},{16,8},{24,16},{0,24},{9,1},{17,9},{25,17},{1,25},{10,2},{18... | collective-permute-start | bytes 38408 | tf_op jit(solution)/shard_map/ppermute | solution.py:20
  5.6 1.3 %fusion.70 = (s32[1]{0:T(128)}, s32[1]{0:T(128)}) fusion(s32[2]{0:T(128)} %param.27), kind=kLoop, calls=%fused_computation.163 | loop fusion | bytes 16 | tf_op jit(solution)/shard_map/slice | solution.py:139
  7.9 2.3 %collective-permute-start.2 = (f32[25,10,1]{2,0,1:T(8,128)S(1)}, f32[25,10,1]{2,0,1:T(8,128)S(1)}, u32[]{:S(2)}, u32[]{:S(2)}) collective-permute-start(f32[25,10,1]{2,0,1:T(8,128)S(1)} %get-tuple-element.206), channel_id=1, source_target_pairs={{0,1},{1,2},{2,3},{3,4},{4,5},{5,6},{6,7},{7,0},{8,9},{9,10},{10,1... | collective-permute-start | bytes 3008 | tf_op jit(solution)/shard_map/ppermute | solution.py:18
  10.2 3.1 %collective-permute-start.3 = (f32[25,10,1]{2,0,1:T(8,128)S(1)}, f32[25,10,1]{2,0,1:T(8,128)S(1)}, u32[]{:S(2)}, u32[]{:S(2)}) collective-permute-start(f32[25,10,1]{2,0,1:T(8,128)S(1)} %get-tuple-element.207), channel_id=1, source_target_pairs={{1,0},{2,1},{3,2},{4,3},{5,4},{6,5},{7,6},{0,7},{9,8},{10,9},{11,1... | collective-permute-start | bytes 3008 | tf_op jit(solution)/shard_map/ppermute | solution.py:20
  14.4 1.3 %copy.212 = f32[2,12,8,128]{1,3,2,0:T(8,128)} copy(f32[2,12,8,128]{3,2,1,0:T(8,128)S(1)} %copy-done.6) | data formatting | bytes 196608 | tf_op args[0]
  15.7 2.6 %collective-permute-done.2 = f32[25,10,1]{2,0,1:T(8,128)S(1)} collective-permute-done((f32[25,10,1]{2,0,1:T(8,128)S(1)}, f32[25,10,1]{2,0,1:T(8,128)S(1)}, u32[]{:S(2)}, u32[]{:S(2)}) %collective-permute-start.2) | collective-permute-done | bytes 1032 | tf_op jit(solution)/shard_map/ppermute | solution.py:18
  18.3 2.1 %collective-permute-done.3 = f32[25,10,1]{2,0,1:T(8,128)S(1)} collective-permute-done((f32[25,10,1]{2,0,1:T(8,128)S(1)}, f32[25,10,1]{2,0,1:T(8,128)S(1)}, u32[]{:S(2)}, u32[]{:S(2)}) %collective-permute-start.3) | collective-permute-done | bytes 1032 | tf_op jit(solution)/shard_map/ppermute | solution.py:20
  20.6 0.5 copy.210
  21.6 2.8 %broadcast_divide_fusion.1 = (f32[2,12,8,128]{1,3,2,0:T(8,128)S(1)}, f32[2,12,8,128]{1,3,2,0:T(8,128)}, f32[2,12,8,128]{1,3,2,0:T(8,128)S(1)}) fusion(f32[8,128]{1,0:T(8,128)S(1)} %get-tuple-element.181, f32[2,12,10,130]{1,3,2,0:T(8,128)S(1)} %scatter.31, f32[8,128]{1,0:T(8,128)S(1)} %get-tuple-element.185, f32[8,128]{1,0:T(8,128)S(1)} %get-tuple-element.184, ...), kind=kLoop, calls=%fused_computation.62 | loop fusion | flops 270336 | bytes 905216 | tf_op jit(solution)/shard_map/div | solution.py:155
  24.4 0.3 copy.214
  24.7 0.3 copy.215
  25.4 1.7 %collective-permute-start.5 = (f32[72,1,128]{2,1,0:T(1,128)S(1)}, f32[72,1,128]{2,1,0:T(1,128)S(1)}, u32[]{:S(2)}, u32[]{:S(2)}) collective-permute-start(f32[72,1,128]{2,1,0:T(1,128)S(1)} %get-tuple-element.205), channel_id=1, source_target_pairs={{8,0},{16,8},{24,16},{0,24},{9,1},{17,9},{25,17},{1,25},{10,2},{18... | collective-permute-start | bytes 110600 | tf_op jit(solution)/shard_map/ppermute | solution.py:20
  27.2 0.6 fusion.47
  27.8 1.0 collective-permute-done.4
  28.9 1.0 fusion.67
  30.0 1.3 %copy.216 = f32[72,10,1]{0,2,1:T(1,128)S(1)} copy(f32[72,10,1]{2,1,0:T(8,128)} %get-tuple-element.202) | data formatting | bytes 5760 | tf_op jit(solution)/shard_map/slice | solution.py:15
  31.2 0.3 collective-permute-start.6
  31.8 4.5 %collective-permute-start.7 = (f32[72,10,1]{0,2,1:T(1,128)S(1)}, f32[72,10,1]{0,2,1:T(1,128)S(1)}, u32[]{:S(2)}, u32[]{:S(2)}) collective-permute-start(f32[72,10,1]{0,2,1:T(1,128)S(1)} %copy.217), channel_id=1, source_target_pairs={{1,0},{2,1},{3,2},{4,3},{5,4},{6,5},{7,6},{0,7},{9,8},{10,9},{11,1... | collective-permute-start | bytes 8648 | tf_op jit(solution)/shard_map/ppermute | solution.py:20
  36.2 1.4 %copy.213 = f32[2,12,8,128]{1,3,2,0:T(8,128)} copy(f32[2,12,8,128]{3,2,1,0:T(8,128)S(1)} %copy-done.5) | data formatting | bytes 196608 | tf_op args[1]
  37.6 0.3 copy.218
  37.9 1.1 copy.219
  39.0 3.0 %pad_maximum_fusion = f32[72,10,130]{2,1,0:T(8,128)} fusion(f32[72,10,1]{2,1,0:T(8,128)} %copy.219, f32[72,1,128]{2,1,0:T(1,128)S(1)} %collective-permute-done.5, f32[72,8,128]{2,1,0:T(8,128)S(1)} %bitcast.123, f32[72,1,128]{2,1,0:T(1,128)S(1)} %collective-permute-done.4, f32[72,10,1]{2,1,0:T(8,128)S(1)} %copy.218), kind=kLoop, calls=%fused_computation.7 | loop fusion | flops 374400 | bytes 748800 | tf_op jit(solution)/shard_map/concatenate | solution.py:16
  42.0 1.8 %copy.223 = f32[2,36,10,130]{1,3,2,0:T(8,128)S(1)} copy(f32[2,36,10,130]{3,2,1,0:T(8,128)} %bitcast.119) | data formatting | bytes 748800 | tf_op jit(solution)/shard_map/reshape | solution.py:161
  44.1 0.2 scatter.39
  44.3 1.8 %fusion.10 = f32[2,36,8,128]{1,3,2,0:T(8,128)S(1)} fusion(f32[2,36,10,130]{1,3,2,0:T(8,128)S(1)} %scatter.39, f32[8,128]{1,0:T(8,128)} %copy-done.8, f32[8,128]{1,0:T(8,128)} %copy-done.7, f32[8,128]{1,0:T(8,128)S(1)} %get-tuple-element.183, f32[8,128]{1,0:T(8,128)S(1)} %get-tuple-element.182, f32[8,128]{1,0:T(8,128)S(1)} %get-tuple-element.181), kind=kLoop, calls=%fused_computation.28 | loop fusion | flops 663552 | bytes 1789952 | tf_op jit(solution)/shard_map/sub | solution.py:58
  46.2 1.1 %pad_maximum_fusion.1 = (f32[2,48,8,128]{1,3,2,0:T(8,128)S(1)}, f32[2,48,8,128]{1,3,2,0:T(8,128)S(1)}) fusion(f32[2,12,8,128]{1,3,2,0:T(8,128)S(1)} %copy-done.3, f32[2,12,8,128]{1,3,2,0:T(8,128)S(1)} %get-tuple-element.210, f32[2,12,8,128]{1,3,2,0:T(8,128)S(1)} %get-tuple-element.179, f32[2,12,8,128]{1,3,2,0:T(8,128)S(1)} %copy-done, ...), kind=kLoop, calls=%fused_computation.44 | loop fusion | flops 393216 | bytes 1572864 | tf_op jit(solution)/shard_map/concatenate | solution.py:166
  47.3 1.1 convolution_bitcast_fusion.2
  48.5 1.0 convolution_bitcast_fusion.4
  49.5 1.1 fusion.5
  50.6 1.0 fusion.6
  51.6 1.8 %convolution_bitcast_fusion.5 = f32[48,48]{1,0:T(8,128)S(1)} fusion(f32[2,48,1024]{1,2,0:T(8,128)S(1)} %bitcast.117), kind=kOutput, calls=%fused_computation.18 | convolution fusion | flops 56623104 | bytes 402432 | tf_op jit(solution)/shard_map/pjc,pkc->jk/dot_general | solution.py:65
  53.4 1.8 %convolution_bitcast_fusion.6 = f32[48,48]{1,0:T(8,128)S(1)} fusion(f32[2,48,1024]{1,2,0:T(8,128)S(1)} %bitcast.118, f32[2,48,1024]{1,2,0:T(8,128)S(1)} %bitcast.120), kind=kOutput, calls=%fused_computation.19 | convolution fusion | flops 56623104 | bytes 795648 | tf_op jit(solution)/shard_map/pjc,pkc->jk/dot_general | solution.py:65
  55.2 40.8 %all-reduce.2 = (f32[48,48]{1,0:T(8,128)S(1)}, f32[48,48]{1,0:T(8,128)S(1)}, f32[48,48]{1,0:T(8,128)S(1)}, f32[48,48]{1,0:T(8,128)S(1)}) all-reduce(f32[48,48]{1,0:T(8,128)S(1)} %convolution_bitcast_fusion.5, f32[48,48]{1,0:T(8,128)S(1)} %convolution_bitcast_fusion.6, ...), channel_id=1, replica_groups=mesh['row'=4,'col'=8] {'row','col'}, use_global_device_ids=true, to_apply=%region_2.3 | all-reduce | flops 9216 | bytes 73728 | tf_op jit(solution)/shard_map/psum | solution.py:170
  96.1 1.0 gather_fusion
  97.0 1.0 gather_fusion.1
  98.1 0.3 fusion.57
  98.4 0.3 fusion.61
  98.7 0.3 fusion.59
  99.0 0.3 fusion.71
  99.3 0.3 fusion.60
  99.6 0.7 multiply_reduce_fusion
  101.1 0.3 fusion.56
  101.5 3.7 %while.21 = (s32[]{:T(128)}, f32[72,72]{0,1:T(8,128)S(1)}, f32[72,72]{1,0:T(8,128)S(1)}, s32[]{:T(128)}) while((s32[]{:T(128)}, f32[72,72]{0,1:T(8,128)S(1)}, f32[72,72]{1,0:T(8,128)S(1)}, s32[]{:T(128)}) %tuple.94), condition=%wide.region_6.7_spmd.clone, body=%wide.region_5.6_spmd.clone.sunk | while | flops 13457666 | bytes 269621 | solution.py:89
  102.0 0.3 convolution_bitcast_fusion.8
  102.7 0.3 convolution_bitcast_fusion.8
  103.5 0.3 convolution_bitcast_fusion.8
  104.2 0.3 convolution_bitcast_fusion.8
  104.9 0.3 convolution_bitcast_fusion.8
  105.9 1.1 copy-done.1
  107.0 0.3 copy-done.4
  107.3 0.6 pad_maximum_fusion.2
  107.9 0.6 fusion.24
  108.5 0.7 fusion.23
  109.2 0.3 fusion.55
  109.5 0.3 fusion.54
  109.8 0.2 convolution_subtract_fusion.2
  111.0 0.6 copy.245
  111.7 0.7 fusion.4
  112.3 0.6 fusion.3
  113.0 0.8 copy.244
  (94 shorter events, 5.7 us)
Async XLA Ops:
  0.6 13.7 %copy-start.6 = (f32[2,12,8,128]{3,2,1,0:T(8,128)S(1)}, f32[2,12,8,128]{3,2,1,0:T(8,128)}, u32[]{:S(2)}) copy-start(f32[2,12,8,128]{3,2,1,0:T(8,128)} %param.23) | copy-start | bytes 294916
  3.1 4.7 %collective-permute-start = (f32[25,1,128]{2,0,1:T(8,128)S(1)}, f32[25,1,128]{2,0,1:T(8,128)S(1)}, u32[]{:S(2)}, u32[]{:S(2)}) collective-permute-start(f32[25,1,128]{2,0,1:T(8,128)S(1)} %get-tuple-element.208), channel_id=1, source_target_pairs={{0,8},{8,16},{16,24},{24,0},{1,9},{9,17},{17,25},{25,1},{2,10},{10... | collective-permute-start | bytes 38408 | tf_op jit(solution)/shard_map/ppermute | solution.py:18
  3.6 4.2 %collective-permute-start.1 = (f32[25,1,128]{2,0,1:T(8,128)S(1)}, f32[25,1,128]{2,0,1:T(8,128)S(1)}, u32[]{:S(2)}, u32[]{:S(2)}) collective-permute-start(f32[25,1,128]{2,0,1:T(8,128)S(1)} %get-tuple-element.209), channel_id=1, source_target_pairs={{8,0},{16,8},{24,16},{0,24},{9,1},{17,9},{25,17},{1,25},{10,2},{18... | collective-permute-start | bytes 38408 | tf_op jit(solution)/shard_map/ppermute | solution.py:20
  7.9 10.3 %collective-permute-start.2 = (f32[25,10,1]{2,0,1:T(8,128)S(1)}, f32[25,10,1]{2,0,1:T(8,128)S(1)}, u32[]{:S(2)}, u32[]{:S(2)}) collective-permute-start(f32[25,10,1]{2,0,1:T(8,128)S(1)} %get-tuple-element.206), channel_id=1, source_target_pairs={{0,1},{1,2},{2,3},{3,4},{4,5},{5,6},{6,7},{7,0},{8,9},{9,10},{10,1... | collective-permute-start | bytes 3008 | tf_op jit(solution)/shard_map/ppermute | solution.py:18
  10.2 10.1 %collective-permute-start.3 = (f32[25,10,1]{2,0,1:T(8,128)S(1)}, f32[25,10,1]{2,0,1:T(8,128)S(1)}, u32[]{:S(2)}, u32[]{:S(2)}) collective-permute-start(f32[25,10,1]{2,0,1:T(8,128)S(1)} %get-tuple-element.207), channel_id=1, source_target_pairs={{1,0},{2,1},{3,2},{4,3},{5,4},{6,5},{7,6},{0,7},{9,8},{10,9},{11,1... | collective-permute-start | bytes 3008 | tf_op jit(solution)/shard_map/ppermute | solution.py:20
  21.5 2.9 %copy-start.7 = (f32[8,128]{1,0:T(8,128)}, f32[8,128]{1,0:T(8,128)S(1)}, u32[]{:S(2)}) copy-start(f32[8,128]{1,0:T(8,128)S(1)} %get-tuple-element.184) | copy-start | bytes 12292
  21.5 2.9 %copy-start.8 = (f32[8,128]{1,0:T(8,128)}, f32[8,128]{1,0:T(8,128)S(1)}, u32[]{:S(2)}) copy-start(f32[8,128]{1,0:T(8,128)S(1)} %get-tuple-element.185) | copy-start | bytes 12292
  24.4 0.9 copy-start.5
  25.4 3.4 %collective-permute-start.4 = (f32[72,1,128]{2,1,0:T(1,128)S(1)}, f32[72,1,128]{2,1,0:T(1,128)S(1)}, u32[]{:S(2)}, u32[]{:S(2)}) collective-permute-start(f32[72,1,128]{2,1,0:T(1,128)S(1)} %get-tuple-element.204), channel_id=1, source_target_pairs={{0,8},{8,16},{16,24},{24,0},{1,9},{9,17},{17,25},{25,1},{2,10},{10... | collective-permute-start | bytes 110600 | tf_op jit(solution)/shard_map/ppermute | solution.py:18
  25.4 3.4 %collective-permute-start.5 = (f32[72,1,128]{2,1,0:T(1,128)S(1)}, f32[72,1,128]{2,1,0:T(1,128)S(1)}, u32[]{:S(2)}, u32[]{:S(2)}) collective-permute-start(f32[72,1,128]{2,1,0:T(1,128)S(1)} %get-tuple-element.205), channel_id=1, source_target_pairs={{8,0},{16,8},{24,16},{0,24},{9,1},{17,9},{25,17},{1,25},{10,2},{18... | collective-permute-start | bytes 110600 | tf_op jit(solution)/shard_map/ppermute | solution.py:20
  31.2 6.4 %collective-permute-start.6 = (f32[72,10,1]{0,2,1:T(1,128)S(1)}, f32[72,10,1]{0,2,1:T(1,128)S(1)}, u32[]{:S(2)}, u32[]{:S(2)}) collective-permute-start(f32[72,10,1]{0,2,1:T(1,128)S(1)} %copy.216), channel_id=1, source_target_pairs={{0,1},{1,2},{2,3},{3,4},{4,5},{5,6},{6,7},{7,0},{8,9},{9,10},{10,1... | collective-permute-start | bytes 8648 | tf_op jit(solution)/shard_map/ppermute | solution.py:18
  31.8 6.2 %collective-permute-start.7 = (f32[72,10,1]{0,2,1:T(1,128)S(1)}, f32[72,10,1]{0,2,1:T(1,128)S(1)}, u32[]{:S(2)}, u32[]{:S(2)}) collective-permute-start(f32[72,10,1]{0,2,1:T(1,128)S(1)} %copy.217), channel_id=1, source_target_pairs={{1,0},{2,1},{3,2},{4,3},{5,4},{6,5},{7,6},{0,7},{9,8},{10,9},{11,1... | collective-permute-start | bytes 8648 | tf_op jit(solution)/shard_map/ppermute | solution.py:20
  44.3 1.8 %copy-start = (f32[2,12,8,128]{1,3,2,0:T(8,128)S(1)}, f32[2,12,8,128]{1,3,2,0:T(8,128)}, u32[]{:S(2)}) copy-start(f32[2,12,8,128]{1,3,2,0:T(8,128)} %copy.212) | copy-start | bytes 294916
  44.3 1.8 %copy-start.2 = (f32[2,12,8,128]{1,3,2,0:T(8,128)S(1)}, f32[2,12,8,128]{1,3,2,0:T(8,128)}, u32[]{:S(2)}) copy-start(f32[2,12,8,128]{1,3,2,0:T(8,128)} %get-tuple-element.180) | copy-start | bytes 294916
  44.3 1.9 %copy-start.3 = (f32[2,12,8,128]{1,3,2,0:T(8,128)S(1)}, f32[2,12,8,128]{1,3,2,0:T(8,128)}, u32[]{:S(2)}) copy-start(f32[2,12,8,128]{1,3,2,0:T(8,128)} %copy.213) | copy-start | bytes 294916
  53.4 44.7 %copy-start.9 = (f32[12,12]{1,0:T(8,128)S(1)}, f32[12,12]{1,0:T(8,128)}, u32[]{:S(2)}) copy-start(f32[12,12]{1,0:T(8,128)} %fusion.47) | copy-start | bytes 1732
  105.7 1.2 %copy-start.1 = (f32[2,12,8,128]{1,3,2,0:T(8,128)S(1)}, f32[2,12,8,128]{1,3,2,0:T(8,128)}, u32[]{:S(2)}) copy-start(f32[2,12,8,128]{1,3,2,0:T(8,128)} %copy.212) | copy-start | bytes 294916
  105.7 1.5 %copy-start.4 = (f32[2,12,8,128]{1,3,2,0:T(8,128)S(1)}, f32[2,12,8,128]{1,3,2,0:T(8,128)}, u32[]{:S(2)}) copy-start(f32[2,12,8,128]{1,3,2,0:T(8,128)} %copy.213) | copy-start | bytes 294916
where the time goes:
time: 114 us
  blocking collectives  40.8 us (36%)
  local copies, waits for them, and re-layouts  17.8 us (16%)
  matrix products  17.8 us (16%)
  starting transfers between devices  14.4 us (13%)
  other arithmetic  13.1 us (11%)
  waiting for transfers between devices  5.71 us (5%)
  between operations  3.93 us (3%)
    psum x1, blocking collectives, body(): lax.psum((local_gram[0], local_gram[1], local_ham[0], local_ham[1]), ('ro...  40.8 us
    ppermute x4, starting transfers between devices, with_halo(): lax.ppermute(head, axis, [((i + 1) % count, i) for i in range(count)])  11.3 us
    unnamed x26, local copies, waits for them, and re-layouts  5.86 us
    ppermute x4, waiting for transfers between devices, with_halo(): lax.ppermute(tail, axis, [(i, (i + 1) % count) for i in range(count)])  3.62 us
    dot_general x2, matrix products, complex_gram(): jnp.einsum('pjc,pkc->jk', first_flat, second_flat, precision=highest)  3.6 us
    concatenate x4, other arithmetic, with_halo(): jnp.concatenate([lax.ppermute(tail, axis, [(i, (i + 1) % count) for i in...  3.24 us
    ppermute x4, starting transfers between devices, with_halo(): lax.ppermute(tail, axis, [(i, (i + 1) % count) for i in range(count)])  3.13 us
    div x1, other arithmetic, body(): applied_cycle / diagonal_cycle  2.78 us
  transfers between devices with their start and end apart: 8, of which 3 were waited for; matrix products, arithmetic and copies ran while one was open for 5% of the time, Pallas kernels for 0%

commit v1 on v0

--- a/solution.py
+++ b/solution.py
@@ -168,7 +168,7 @@
     local_gram = complex_gram(extended, extended)
     local_ham = complex_gram(extended, extended_applied)
     gram_whole, gram_imag_whole, ham_whole, ham_imag_whole = lax.psum(
-        (local_gram[0], local_gram[1], local_ham[0], local_ham[1]), ("row", "col")
+        lax.psum((local_gram[0], local_gram[1], local_ham[0], local_ham[1]), "col"), "row"
     )
     quotient = jnp.diagonal(ham_whole)[:band_count] / jnp.diagonal(gram_whole)[:band_count]
     identity = jnp.eye(band_count, dtype=jnp.float32)

time: 114 us -> 124 us (1.088)
  blocking collectives: 40.8 us -> 50 us
    psum x1 -> x2, blocking collectives: 40.8 us -> 50 us  [the longest x1 38.7 us: body(): lax.psum((local_gram[0], local_gram[1], local_ham[0], local_ham[1]), 'col')]
  transfers between devices with their start and end apart: 8 -> 8, of which waited for: 3 -> 3; matrix products, arithmetic and copies ran while one was open for 5% -> 4% of each run, Pallas kernels for 0% -> 0%
where the time goes in v1:
time: 124 us; the launch traced here: 123 us
  blocking collectives  50 us (40%)
  local copies, waits for them, and re-layouts  17.8 us (14%)
  matrix products  17.8 us (14%)
  starting transfers between devices  14.4 us (12%)
  other arithmetic  13.1 us (11%)
  waiting for transfers between devices  5.69 us (5%)
  between operations  3.93 us (3%)
    psum x1, blocking collectives, body(): lax.psum((local_gram[0], local_gram[1], local_ham[0], local_ham[1]), 'col')  38.7 us
    psum x1, blocking collectives, body(): lax.psum(lax.psum((local_gram[0], local_gram[1], local_ham[0], local_ham[...  11.3 us
    ppermute x4, starting transfers between devices, with_halo(): lax.ppermute(head, axis, [((i + 1) % count, i) for i in range(count)])  11.3 us
    unnamed x26, local copies, waits for them, and re-layouts  5.89 us
    ppermute x4, waiting for transfers between devices, with_halo(): lax.ppermute(tail, axis, [(i, (i + 1) % count) for i in range(count)])  3.61 us
    dot_general x2, matrix products, complex_gram(): jnp.einsum('pjc,pkc->jk', first_flat, second_flat, precision=highest)  3.6 us
    concatenate x4, other arithmetic, with_halo(): jnp.concatenate([lax.ppermute(tail, axis, [(i, (i + 1) % count) for i in...  3.24 us
    ppermute x4, starting transfers between devices, with_halo(): lax.ppermute(tail, axis, [(i, (i + 1) % count) for i in range(count)])  3.13 us
  transfers between devices with their start and end apart: 8, of which 3 were waited for; matrix products, arithmetic and copies ran while one was open for 4% of the time, Pallas kernels for 0%

profile of v1, /device:TPU:0, one launch (start us, length us, event | category | flops | bytes accessed | tf_op | source)
XLA Modules:
  0.0 123.0 jit_solution(14664520803353210474)
XLA Ops:
  0.6 1.0 copy.206
  1.6 0.7 broadcast_divide_fusion.4
  2.3 0.8 select_reduce_fusion
  3.1 0.5 collective-permute-start
  3.6 2.0 %collective-permute-start.1 = (f32[25,1,128]{2,0,1:T(8,128)S(1)}, f32[25,1,128]{2,0,1:T(8,128)S(1)}, u32[]{:S(2)}, u32[]{:S(2)}) collective-permute-start(f32[25,1,128]{2,0,1:T(8,128)S(1)} %get-tuple-element.213), channel_id=1, source_target_pairs={{8,0},{16,8},{24,16},{0,24},{9,1},{17,9},{25,17},{1,25},{10,2},{18... | collective-permute-start | bytes 38408 | tf_op jit(solution)/shard_map/ppermute | solution.py:20
  5.6 1.3 %fusion.70 = (s32[1]{0:T(128)}, s32[1]{0:T(128)}) fusion(s32[2]{0:T(128)} %param.27), kind=kLoop, calls=%fused_computation.163 | loop fusion | bytes 16 | tf_op jit(solution)/shard_map/slice | solution.py:139
  7.9 2.3 %collective-permute-start.2 = (f32[25,10,1]{2,0,1:T(8,128)S(1)}, f32[25,10,1]{2,0,1:T(8,128)S(1)}, u32[]{:S(2)}, u32[]{:S(2)}) collective-permute-start(f32[25,10,1]{2,0,1:T(8,128)S(1)} %get-tuple-element.210), channel_id=1, source_target_pairs={{0,1},{1,2},{2,3},{3,4},{4,5},{5,6},{6,7},{7,0},{8,9},{9,10},{10,1... | collective-permute-start | bytes 3008 | tf_op jit(solution)/shard_map/ppermute | solution.py:18
  10.2 3.1 %collective-permute-start.3 = (f32[25,10,1]{2,0,1:T(8,128)S(1)}, f32[25,10,1]{2,0,1:T(8,128)S(1)}, u32[]{:S(2)}, u32[]{:S(2)}) collective-permute-start(f32[25,10,1]{2,0,1:T(8,128)S(1)} %get-tuple-element.211), channel_id=1, source_target_pairs={{1,0},{2,1},{3,2},{4,3},{5,4},{6,5},{7,6},{0,7},{9,8},{10,9},{11,1... | collective-permute-start | bytes 3008 | tf_op jit(solution)/shard_map/ppermute | solution.py:20
  14.4 1.3 %copy.212 = f32[2,12,8,128]{1,3,2,0:T(8,128)} copy(f32[2,12,8,128]{3,2,1,0:T(8,128)S(1)} %copy-done.6) | data formatting | bytes 196608 | tf_op args[0]
  15.7 2.6 %collective-permute-done.2 = f32[25,10,1]{2,0,1:T(8,128)S(1)} collective-permute-done((f32[25,10,1]{2,0,1:T(8,128)S(1)}, f32[25,10,1]{2,0,1:T(8,128)S(1)}, u32[]{:S(2)}, u32[]{:S(2)}) %collective-permute-start.2) | collective-permute-done | bytes 1032 | tf_op jit(solution)/shard_map/ppermute | solution.py:18
  18.3 2.1 %collective-permute-done.3 = f32[25,10,1]{2,0,1:T(8,128)S(1)} collective-permute-done((f32[25,10,1]{2,0,1:T(8,128)S(1)}, f32[25,10,1]{2,0,1:T(8,128)S(1)}, u32[]{:S(2)}, u32[]{:S(2)}) %collective-permute-start.3) | collective-permute-done | bytes 1032 | tf_op jit(solution)/shard_map/ppermute | solution.py:20
  20.6 0.5 copy.210
  21.6 2.8 %broadcast_divide_fusion.1 = (f32[2,12,8,128]{1,3,2,0:T(8,128)S(1)}, f32[2,12,8,128]{1,3,2,0:T(8,128)}, f32[2,12,8,128]{1,3,2,0:T(8,128)S(1)}) fusion(f32[8,128]{1,0:T(8,128)S(1)} %get-tuple-element.185, f32[2,12,10,130]{1,3,2,0:T(8,128)S(1)} %scatter.31, f32[8,128]{1,0:T(8,128)S(1)} %get-tuple-element.189, f32[8,128]{1,0:T(8,128)S(1)} %get-tuple-element.188, ...), kind=kLoop, calls=%fused_computation.62 | loop fusion | flops 270336 | bytes 905216 | tf_op jit(solution)/shard_map/div | solution.py:155
  24.4 0.3 copy.214
  24.7 0.3 copy.215
  25.4 1.7 %collective-permute-start.5 = (f32[72,1,128]{2,1,0:T(1,128)S(1)}, f32[72,1,128]{2,1,0:T(1,128)S(1)}, u32[]{:S(2)}, u32[]{:S(2)}) collective-permute-start(f32[72,1,128]{2,1,0:T(1,128)S(1)} %get-tuple-element.209), channel_id=1, source_target_pairs={{8,0},{16,8},{24,16},{0,24},{9,1},{17,9},{25,17},{1,25},{10,2},{18... | collective-permute-start | bytes 110600 | tf_op jit(solution)/shard_map/ppermute | solution.py:20
  27.2 0.6 fusion.47
  27.8 1.0 collective-permute-done.4
  28.9 1.1 fusion.67
  30.0 1.3 %copy.216 = f32[72,10,1]{0,2,1:T(1,128)S(1)} copy(f32[72,10,1]{2,1,0:T(8,128)} %get-tuple-element.206) | data formatting | bytes 5760 | tf_op jit(solution)/shard_map/slice | solution.py:15
  31.2 0.3 collective-permute-start.6
  31.8 4.5 %collective-permute-start.7 = (f32[72,10,1]{0,2,1:T(1,128)S(1)}, f32[72,10,1]{0,2,1:T(1,128)S(1)}, u32[]{:S(2)}, u32[]{:S(2)}) collective-permute-start(f32[72,10,1]{0,2,1:T(1,128)S(1)} %copy.217), channel_id=1, source_target_pairs={{1,0},{2,1},{3,2},{4,3},{5,4},{6,5},{7,6},{0,7},{9,8},{10,9},{11,1... | collective-permute-start | bytes 8648 | tf_op jit(solution)/shard_map/ppermute | solution.py:20
  36.2 1.4 %copy.213 = f32[2,12,8,128]{1,3,2,0:T(8,128)} copy(f32[2,12,8,128]{3,2,1,0:T(8,128)S(1)} %copy-done.5) | data formatting | bytes 196608 | tf_op args[1]
  37.6 0.3 copy.218
  38.0 1.1 copy.219
  39.1 3.0 %pad_maximum_fusion = f32[72,10,130]{2,1,0:T(8,128)} fusion(f32[72,10,1]{2,1,0:T(8,128)} %copy.219, f32[72,1,128]{2,1,0:T(1,128)S(1)} %collective-permute-done.5, f32[72,8,128]{2,1,0:T(8,128)S(1)} %bitcast.123, f32[72,1,128]{2,1,0:T(1,128)S(1)} %collective-permute-done.4, f32[72,10,1]{2,1,0:T(8,128)S(1)} %copy.218), kind=kLoop, calls=%fused_computation.7 | loop fusion | flops 374400 | bytes 748800 | tf_op jit(solution)/shard_map/concatenate | solution.py:16
  42.0 1.8 %copy.223 = f32[2,36,10,130]{1,3,2,0:T(8,128)S(1)} copy(f32[2,36,10,130]{3,2,1,0:T(8,128)} %bitcast.119) | data formatting | bytes 748800 | tf_op jit(solution)/shard_map/reshape | solution.py:161
  44.1 0.2 scatter.39
  44.4 1.8 %fusion.10 = f32[2,36,8,128]{1,3,2,0:T(8,128)S(1)} fusion(f32[2,36,10,130]{1,3,2,0:T(8,128)S(1)} %scatter.39, f32[8,128]{1,0:T(8,128)} %copy-done.8, f32[8,128]{1,0:T(8,128)} %copy-done.7, f32[8,128]{1,0:T(8,128)S(1)} %get-tuple-element.187, f32[8,128]{1,0:T(8,128)S(1)} %get-tuple-element.186, f32[8,128]{1,0:T(8,128)S(1)} %get-tuple-element.185), kind=kLoop, calls=%fused_computation.28 | loop fusion | flops 663552 | bytes 1789952 | tf_op jit(solution)/shard_map/sub | solution.py:58
  46.2 1.1 pad_maximum_fusion.1
  47.4 1.1 convolution_bitcast_fusion.2
  48.5 1.0 convolution_bitcast_fusion.4
  49.5 1.1 fusion.5
  50.7 1.0 fusion.6
  51.7 1.8 %convolution_bitcast_fusion.5 = f32[48,48]{1,0:T(8,128)S(1)} fusion(f32[2,48,1024]{1,2,0:T(8,128)S(1)} %bitcast.117), kind=kOutput, calls=%fused_computation.18 | convolution fusion | flops 56623104 | bytes 402432 | tf_op jit(solution)/shard_map/pjc,pkc->jk/dot_general | solution.py:65
  53.5 1.8 %convolution_bitcast_fusion.6 = f32[48,48]{1,0:T(8,128)S(1)} fusion(f32[2,48,1024]{1,2,0:T(8,128)S(1)} %bitcast.118, f32[2,48,1024]{1,2,0:T(8,128)S(1)} %bitcast.120), kind=kOutput, calls=%fused_computation.19 | convolution fusion | flops 56623104 | bytes 795648 | tf_op jit(solution)/shard_map/pjc,pkc->jk/dot_general | solution.py:65
  55.3 38.7 %all-reduce.2 = (f32[48,48]{1,0:T(8,128)S(1)}, f32[48,48]{1,0:T(8,128)S(1)}, f32[48,48]{1,0:T(8,128)S(1)}, f32[48,48]{1,0:T(8,128)S(1)}) all-reduce(f32[48,48]{1,0:T(8,128)S(1)} %convolution_bitcast_fusion.5, f32[48,48]{1,0:T(8,128)S(1)} %convolution_bitcast_fusion.6, ...), channel_id=1, replica_groups=mesh['row'=4,'col'=8] {'col'}, use_global_device_ids=true, to_apply=%region_3.4 | all-reduce | flops 9216 | bytes 73728 | tf_op jit(solution)/shard_map/psum | solution.py:171
  94.0 11.3 %all-reduce.3 = (f32[48,48]{1,0:T(8,128)S(1)}, f32[48,48]{1,0:T(8,128)S(1)}, f32[48,48]{1,0:T(8,128)S(1)}, f32[48,48]{1,0:T(8,128)S(1)}) all-reduce(f32[48,48]{1,0:T(8,128)S(1)} %get-tuple-element.175, f32[48,48]{1,0:T(8,128)S(1)} %get-tuple-element.176, ...), channel_id=1, replica_groups=mesh['row'=4,'col'=8] {'row'}, use_global_device_ids=true, to_apply=%region_4.5 | all-reduce | flops 9216 | bytes 73728 | tf_op jit(solution)/shard_map/psum | solution.py:170
  105.3 1.0 gather_fusion
  106.3 1.0 gather_fusion.1
  107.3 0.3 fusion.57
  107.6 0.3 fusion.61
  107.9 0.3 fusion.59
  108.3 0.3 fusion.71
  108.6 0.3 fusion.60
  108.9 0.7 multiply_reduce_fusion
  110.4 0.3 fusion.56
  110.8 3.7 %while.21 = (s32[]{:T(128)}, f32[72,72]{0,1:T(8,128)S(1)}, f32[72,72]{1,0:T(8,128)S(1)}, s32[]{:T(128)}) while((s32[]{:T(128)}, f32[72,72]{0,1:T(8,128)S(1)}, f32[72,72]{1,0:T(8,128)S(1)}, s32[]{:T(128)}) %tuple.94), condition=%wide.region_9.10_spmd.clone, body=%wide.region_8.9_spmd.clone.sunk | while | flops 13457666 | bytes 269621 | solution.py:89
  111.2 0.3 convolution_bitcast_fusion.8
  112.0 0.3 convolution_bitcast_fusion.8
  112.7 0.3 convolution_bitcast_fusion.8
  113.4 0.3 convolution_bitcast_fusion.8
  114.2 0.3 convolution_bitcast_fusion.8
  115.1 1.1 copy-done.1
  116.2 0.3 copy-done.4
  116.5 0.6 pad_maximum_fusion.2
  117.1 0.6 fusion.24
  117.8 0.7 fusion.23
  118.4 0.3 fusion.55
  118.7 0.3 fusion.54
  120.3 0.6 copy.245
  120.9 0.7 fusion.4
  121.6 0.6 fusion.3
  122.3 0.8 copy.244
  (95 shorter events, 6.0 us)
Async XLA Ops:
  0.6 13.7 %copy-start.6 = (f32[2,12,8,128]{3,2,1,0:T(8,128)S(1)}, f32[2,12,8,128]{3,2,1,0:T(8,128)}, u32[]{:S(2)}) copy-start(f32[2,12,8,128]{3,2,1,0:T(8,128)} %param.23) | copy-start | bytes 294916
  3.1 4.7 %collective-permute-start = (f32[25,1,128]{2,0,1:T(8,128)S(1)}, f32[25,1,128]{2,0,1:T(8,128)S(1)}, u32[]{:S(2)}, u32[]{:S(2)}) collective-permute-start(f32[25,1,128]{2,0,1:T(8,128)S(1)} %get-tuple-element.212), channel_id=1, source_target_pairs={{0,8},{8,16},{16,24},{24,0},{1,9},{9,17},{17,25},{25,1},{2,10},{10... | collective-permute-start | bytes 38408 | tf_op jit(solution)/shard_map/ppermute | solution.py:18
  3.6 4.2 %collective-permute-start.1 = (f32[25,1,128]{2,0,1:T(8,128)S(1)}, f32[25,1,128]{2,0,1:T(8,128)S(1)}, u32[]{:S(2)}, u32[]{:S(2)}) collective-permute-start(f32[25,1,128]{2,0,1:T(8,128)S(1)} %get-tuple-element.213), channel_id=1, source_target_pairs={{8,0},{16,8},{24,16},{0,24},{9,1},{17,9},{25,17},{1,25},{10,2},{18... | collective-permute-start | bytes 38408 | tf_op jit(solution)/shard_map/ppermute | solution.py:20
  7.9 10.3 %collective-permute-start.2 = (f32[25,10,1]{2,0,1:T(8,128)S(1)}, f32[25,10,1]{2,0,1:T(8,128)S(1)}, u32[]{:S(2)}, u32[]{:S(2)}) collective-permute-start(f32[25,10,1]{2,0,1:T(8,128)S(1)} %get-tuple-element.210), channel_id=1, source_target_pairs={{0,1},{1,2},{2,3},{3,4},{4,5},{5,6},{6,7},{7,0},{8,9},{9,10},{10,1... | collective-permute-start | bytes 3008 | tf_op jit(solution)/shard_map/ppermute | solution.py:18
  10.2 10.1 %collective-permute-start.3 = (f32[25,10,1]{2,0,1:T(8,128)S(1)}, f32[25,10,1]{2,0,1:T(8,128)S(1)}, u32[]{:S(2)}, u32[]{:S(2)}) collective-permute-start(f32[25,10,1]{2,0,1:T(8,128)S(1)} %get-tuple-element.211), channel_id=1, source_target_pairs={{1,0},{2,1},{3,2},{4,3},{5,4},{6,5},{7,6},{0,7},{9,8},{10,9},{11,1... | collective-permute-start | bytes 3008 | tf_op jit(solution)/shard_map/ppermute | solution.py:20
  21.5 2.9 %copy-start.7 = (f32[8,128]{1,0:T(8,128)}, f32[8,128]{1,0:T(8,128)S(1)}, u32[]{:S(2)}) copy-start(f32[8,128]{1,0:T(8,128)S(1)} %get-tuple-element.188) | copy-start | bytes 12292
  21.5 2.9 %copy-start.8 = (f32[8,128]{1,0:T(8,128)}, f32[8,128]{1,0:T(8,128)S(1)}, u32[]{:S(2)}) copy-start(f32[8,128]{1,0:T(8,128)S(1)} %get-tuple-element.189) | copy-start | bytes 12292
  24.4 0.9 copy-start.5
  25.4 3.4 %collective-permute-start.4 = (f32[72,1,128]{2,1,0:T(1,128)S(1)}, f32[72,1,128]{2,1,0:T(1,128)S(1)}, u32[]{:S(2)}, u32[]{:S(2)}) collective-permute-start(f32[72,1,128]{2,1,0:T(1,128)S(1)} %get-tuple-element.208), channel_id=1, source_target_pairs={{0,8},{8,16},{16,24},{24,0},{1,9},{9,17},{17,25},{25,1},{2,10},{10... | collective-permute-start | bytes 110600 | tf_op jit(solution)/shard_map/ppermute | solution.py:18
  25.4 3.4 %collective-permute-start.5 = (f32[72,1,128]{2,1,0:T(1,128)S(1)}, f32[72,1,128]{2,1,0:T(1,128)S(1)}, u32[]{:S(2)}, u32[]{:S(2)}) collective-permute-start(f32[72,1,128]{2,1,0:T(1,128)S(1)} %get-tuple-element.209), channel_id=1, source_target_pairs={{8,0},{16,8},{24,16},{0,24},{9,1},{17,9},{25,17},{1,25},{10,2},{18... | collective-permute-start | bytes 110600 | tf_op jit(solution)/shard_map/ppermute | solution.py:20
  31.2 6.4 %collective-permute-start.6 = (f32[72,10,1]{0,2,1:T(1,128)S(1)}, f32[72,10,1]{0,2,1:T(1,128)S(1)}, u32[]{:S(2)}, u32[]{:S(2)}) collective-permute-start(f32[72,10,1]{0,2,1:T(1,128)S(1)} %copy.216), channel_id=1, source_target_pairs={{0,1},{1,2},{2,3},{3,4},{4,5},{5,6},{6,7},{7,0},{8,9},{9,10},{10,1... | collective-permute-start | bytes 8648 | tf_op jit(solution)/shard_map/ppermute | solution.py:18
  31.8 6.2 %collective-permute-start.7 = (f32[72,10,1]{0,2,1:T(1,128)S(1)}, f32[72,10,1]{0,2,1:T(1,128)S(1)}, u32[]{:S(2)}, u32[]{:S(2)}) collective-permute-start(f32[72,10,1]{0,2,1:T(1,128)S(1)} %copy.217), channel_id=1, source_target_pairs={{1,0},{2,1},{3,2},{4,3},{5,4},{6,5},{7,6},{0,7},{9,8},{10,9},{11,1... | collective-permute-start | bytes 8648 | tf_op jit(solution)/shard_map/ppermute | solution.py:20
  44.4 1.8 %copy-start = (f32[2,12,8,128]{1,3,2,0:T(8,128)S(1)}, f32[2,12,8,128]{1,3,2,0:T(8,128)}, u32[]{:S(2)}) copy-start(f32[2,12,8,128]{1,3,2,0:T(8,128)} %copy.212) | copy-start | bytes 294916
  44.4 1.8 %copy-start.2 = (f32[2,12,8,128]{1,3,2,0:T(8,128)S(1)}, f32[2,12,8,128]{1,3,2,0:T(8,128)}, u32[]{:S(2)}) copy-start(f32[2,12,8,128]{1,3,2,0:T(8,128)} %get-tuple-element.184) | copy-start | bytes 294916
  44.4 1.9 %copy-start.3 = (f32[2,12,8,128]{1,3,2,0:T(8,128)S(1)}, f32[2,12,8,128]{1,3,2,0:T(8,128)}, u32[]{:S(2)}) copy-start(f32[2,12,8,128]{1,3,2,0:T(8,128)} %copy.213) | copy-start | bytes 294916
  53.5 53.8 %copy-start.9 = (f32[12,12]{1,0:T(8,128)S(1)}, f32[12,12]{1,0:T(8,128)}, u32[]{:S(2)}) copy-start(f32[12,12]{1,0:T(8,128)} %fusion.47) | copy-start | bytes 1732
  115.0 1.2 copy-start.1
  115.0 1.5 %copy-start.4 = (f32[2,12,8,128]{1,3,2,0:T(8,128)S(1)}, f32[2,12,8,128]{1,3,2,0:T(8,128)}, u32[]{:S(2)}) copy-start(f32[2,12,8,128]{1,3,2,0:T(8,128)} %copy.213) | copy-start | bytes 294916
